TPU v7x, 256 devices: a whole 4x4x8 slice. The times are simulated.
256 devices in a mesh: dp: 4 (over x), expert: 64 (over z, y, core).
Axes of the slice: x: 4, y: 4, z: 8, core: 2. Of those that a mesh axis runs over, the one named last changes fastest.
Arguments:
- tokens: bfloat16 [32768, 4096], P(('dp', 'expert')), may hold values from -6 to 6
- out_grad: bfloat16 [32768, 4096], P(('dp', 'expert')), may hold values from -0.75 to 0.75
- routes: int32 [32768, 1], P(('dp', 'expert')), may hold values from 0 to 63; in each aligned block of 128 rows (0 to 127, 128 to 255, ...) at most 3 rows name the same one
- gate_probs: bfloat16 [32768, 1], P(('dp', 'expert')), may hold values from 0.049804688 to 1
- w_gate: bfloat16 [64, 4096, 768], P('expert', None, 'dp'), may hold values from -0.09375 to 0.09375
- w_up: bfloat16 [64, 4096, 768], P('expert', None, 'dp'), may hold values from -0.09375 to 0.09375
- w_down: bfloat16 [64, 768, 4096], P('expert', 'dp'), may hold values from -0.21875 to 0.21875
Outputs:
- grad_tokens: bfloat16 [32768, 4096], P(('dp', 'expert'))
- grad_probs: bfloat16 [32768, 1], P(('dp', 'expert'))
- grad_w_gate: bfloat16 [64, 4096, 768], P('expert', None, 'dp')
- grad_w_up: bfloat16 [64, 4096, 768], P('expert', None, 'dp')
- grad_w_down: bfloat16 [64, 768, 4096], P('expert', 'dp')
Inputs may be any that keep to these rules, and one draw needn't show every extreme that they name: `routes`: the experts of one token are different. Among the 128 tokens of one device no expert is named more than 3 times, a bound that some block reaches.
All inputs are finite; a program needn't handle non-finite values.
Results may differ from a plain program's by a relative error of at most 0.018.
Values may be sent and summed in bfloat16 or wider, within the bound.
No kernel may reach another device: no remote copies, remote signals or barrier semaphores. Data moves between devices by JAX's collectives and lax.ppermute only.
A program may use at most 128 MiB of HBM per device.

v0:
```python
import jax
import jax.numpy as jnp
from jax import lax
from jax.sharding import PartitionSpec as P

LANES = 128
CHUNKS = 2


def body(tokens, out_grad, routes, gate_probs, w_gate, w_up, w_down):
    expert_count = lax.axis_size("expert")
    tok_count, width = tokens.shape
    top_count = routes.shape[1]
    capacity = 3 * tok_count * top_count // (2 * expert_count)
    slot_total = expert_count * capacity
    piece = width // CHUNKS
    per_peer = capacity * piece // LANES
    flat_routes = routes.reshape(-1)
    one_hot = (flat_routes[:, None] == jnp.arange(expert_count, dtype=jnp.int32)[None, :]).astype(
        jnp.int32
    )
    earlier = jnp.cumsum(one_hot, axis=0) - one_hot
    slot_index = jnp.sum(earlier * one_hot, axis=1)
    destination = flat_routes * capacity + slot_index
    placing = (jnp.arange(slot_total, dtype=jnp.int32)[:, None] == destination[None, :]).astype(
        jnp.bfloat16
    )
    collect = jnp.sum(placing.reshape(slot_total, tok_count, top_count), axis=2)
    contract_last = (((1,), (1,)), ((), ()))
    contract_first = (((0,), (0,)), ((), ()))

    def to_expert(rows):
        shaped = rows.reshape(expert_count, per_peer, LANES)
        return lax.all_to_all(shaped, "expert", 0, 0, tiled=True).reshape(slot_total, piece)

    def dispatch(source, c):
        part = source[:, c * piece : (c + 1) * piece]
        rows = jnp.dot(collect, part, preferred_element_type=jnp.float32).astype(jnp.bfloat16)
        return to_expert(rows)

    sent_prob = (
        jnp.dot(placing, gate_probs.reshape(-1), preferred_element_type=jnp.float32)
        .astype(jnp.bfloat16)
        .reshape(expert_count, capacity)
    )
    recv_prob = lax.all_to_all(sent_prob, "expert", 0, 0, tiled=True).reshape(slot_total)
    rows_in = []
    for c in range(CHUNKS):
        rows_in.append(lax.all_gather(dispatch(tokens, c), "dp", axis=0, tiled=True))
    rows_dy = []
    rows_prob = None
    for c in range(CHUNKS):
        recv = dispatch(out_grad, c)
        if c == 0:
            recv = jnp.concatenate(
                [recv, jnp.broadcast_to(recv_prob[:, None], (slot_total, LANES))], axis=1
            )
        gathered = lax.all_gather(recv, "dp", axis=0, tiled=True)
        if c == 0:
            rows_prob = gathered[:, piece]
            gathered = gathered[:, :piece]
        rows_dy.append(gathered)
    gate_w = w_gate[0]
    up_w = w_up[0]
    down_w = w_down[0]
    gate_pre = None
    up_pre = None
    for c in range(CHUNKS):
        g = jnp.dot(
            rows_in[c], gate_w[c * piece : (c + 1) * piece], preferred_element_type=jnp.float32
        )
        u = jnp.dot(
            rows_in[c], up_w[c * piece : (c + 1) * piece], preferred_element_type=jnp.float32
        )
        gate_pre = g if gate_pre is None else gate_pre + g
        up_pre = u if up_pre is None else up_pre + u
    sigmoid_gate = jax.nn.sigmoid(gate_pre)
    active = gate_pre * sigmoid_gate
    hidden = (active * up_pre).astype(jnp.bfloat16)
    back_raw = None
    for c in range(CHUNKS):
        b = lax.dot_general(
            rows_dy[c],
            down_w[:, c * piece : (c + 1) * piece],
            contract_last,
            preferred_element_type=jnp.float32,
        )
        back_raw = b if back_raw is None else back_raw + b
    score_part = jnp.sum(back_raw * hidden.astype(jnp.float32), axis=1)
    weight_col = rows_prob.astype(jnp.float32)[:, None]
    back_hidden = weight_col * back_raw
    grad_gate_pre = (
        back_hidden * up_pre * sigmoid_gate * (1.0 + gate_pre * (1.0 - sigmoid_gate))
    ).astype(jnp.bfloat16)
    grad_up_pre = (back_hidden * active).astype(jnp.bfloat16)
    row_total = grad_gate_pre.shape[0]
    back_rows = []
    back_scores = None
    for c in range(CHUNKS):
        part = lax.dot_general(
            grad_gate_pre,
            gate_w[c * piece : (c + 1) * piece],
            contract_last,
            preferred_element_type=jnp.float32,
        )
        part = part + lax.dot_general(
            grad_up_pre,
            up_w[c * piece : (c + 1) * piece],
            contract_last,
            preferred_element_type=jnp.float32,
        )
        if c == 0:
            part = jnp.concatenate(
                [part, jnp.broadcast_to(score_part[:, None], (row_total, LANES))], axis=1
            )
        own = lax.psum_scatter(part.astype(jnp.bfloat16), "dp", scatter_dimension=0, tiled=True)
        if c == 0:
            own_scores = own[:, piece].reshape(expert_count, capacity)
            back_scores = lax.all_to_all(own_scores, "expert", 0, 0, tiled=True).reshape(slot_total)
            own = own[:, :piece]
        back_rows.append(to_expert(own))
    grad_down = []
    grad_gate = []
    grad_up = []
    for c in range(CHUNKS):
        dy_c = rows_dy[c]
        scaled = (weight_col * dy_c.astype(jnp.float32)).astype(jnp.bfloat16)
        grad_down.append(
            lax.dot_general(
                hidden, scaled, contract_first, preferred_element_type=jnp.float32
            ).astype(jnp.bfloat16)
        )
        grad_gate.append(
            lax.dot_general(
                rows_in[c], grad_gate_pre, contract_first, preferred_element_type=jnp.float32
            ).astype(jnp.bfloat16)
        )
        grad_up.append(
            lax.dot_general(
                rows_in[c], grad_up_pre, contract_first, preferred_element_type=jnp.float32
            ).astype(jnp.bfloat16)
        )
    grad_down = jnp.concatenate(grad_down, axis=1)
    grad_gate = jnp.concatenate(grad_gate, axis=0)
    grad_up = jnp.concatenate(grad_up, axis=0)
    grad_tokens = jnp.concatenate(
        [
            lax.dot_general(
                collect, back_rows[c], contract_first, preferred_element_type=jnp.float32
            ).astype(jnp.bfloat16)
            for c in range(CHUNKS)
        ],
        axis=1,
    )
    grad_probs = (
        jnp.dot(back_scores, placing, preferred_element_type=jnp.float32)
        .astype(jnp.bfloat16)
        .reshape(tok_count, top_count)
    )
    return (grad_tokens, grad_probs, grad_gate[None], grad_up[None], grad_down[None])


def solution(mesh):
    in_specs = (
        P(("dp", "expert"), None),
        P(("dp", "expert"), None),
        P(("dp", "expert"), None),
        P(("dp", "expert"), None),
        P("expert", None, "dp"),
        P("expert", None, "dp"),
        P("expert", "dp", None),
    )
    out_specs = (
        P(("dp", "expert"), None),
        P(("dp", "expert"), None),
        P("expert", None, "dp"),
        P("expert", None, "dp"),
        P("expert", "dp", None),
    )
    return jax.shard_map(body, mesh=mesh, in_specs=in_specs, out_specs=out_specs, check_vma=False)
```

profile of v0, /device:TPU:1, one launch (start us, length us, event | category | flops | bytes accessed | tf_op | source)
XLA Modules:
  0.0 393.0 jit_solution(721865889223023181)
XLA Ops:
  11.5 35.9 %all_to_all.50 = bf16[64,48,128]{2,1,0:T(8,128)(2,1)S(1)} all-to-all(bf16[64,48,128]{2,1,0:T(8,128)(2,1)S(1)} %reshape.110), channel_id=1, replica_groups=mesh['dp'=4,'expert'=64] {'expert'}, dimensions={0} | all-to-all | bytes 1572864 | tf_op jit(solution)/shard_map/all_to_all | solution.py:34
  49.5 28.7 %all_to_all.51 = bf16[64,48,128]{2,1,0:T(8,128)(2,1)S(1)} all-to-all(bf16[64,48,128]{2,1,0:T(8,128)(2,1)S(1)} %reshape.112), channel_id=1, replica_groups=mesh['dp'=4,'expert'=64] {'expert'}, dimensions={0} | all-to-all | bytes 1572864 | tf_op jit(solution)/shard_map/all_to_all | solution.py:34
  80.4 5.9 %all-to-all-start.1 = ((bf16[64,1,3]{2,1,0:T(2,128)(2,1)}), bf16[64,1,3]{2,1,0:T(2,128)(2,1)S(1)}, u32[]{:S(2)}, u32[]{:S(2)}) async-start(bf16[64,1,3]{2,1,0:T(2,128)(2,1)} %all_to_all.40), calls=%async_computation.1 | async-start | bytes 65536 | tf_op jit(solution)/shard_map/all_to_all | solution.py:46
  87.9 7.7 %all-to-all-done.1 = bf16[64,1,3]{2,1,0:T(2,128)(2,1)S(1)} async-done(((bf16[64,1,3]{2,1,0:T(2,128)(2,1)}), bf16[64,1,3]{2,1,0:T(2,128)(2,1)S(1)}, u32[]{:S(2)}, u32[]{:S(2)}) %all-to-all-start.1) | async-done | bytes 416 | tf_op jit(solution)/shard_map/all_to_all | solution.py:46
  95.7 4.8 %all-to-all-start = ((bf16[64,48,128]{2,1,0:T(8,128)(2,1)}), bf16[64,48,128]{2,1,0:T(8,128)(2,1)S(1)}, u32[]{:S(2)}, u32[]{:S(2)}) async-start(bf16[64,48,128]{2,1,0:T(8,128)(2,1)} %reshape.105), calls=%async_computation | async-start | bytes 1572864 | tf_op jit(solution)/shard_map/all_to_all | solution.py:34
  100.7 22.9 %all-to-all-done = bf16[64,48,128]{2,1,0:T(8,128)(2,1)S(1)} async-done(((bf16[64,48,128]{2,1,0:T(8,128)(2,1)}), bf16[64,48,128]{2,1,0:T(8,128)(2,1)S(1)}, u32[]{:S(2)}, u32[]{:S(2)}) %all-to-all-start) | async-done | bytes 786464 | tf_op jit(solution)/shard_map/all_to_all | solution.py:34
  127.0 28.6 %all_to_all.52 = bf16[64,48,128]{2,1,0:T(8,128)(2,1)S(1)} all-to-all(bf16[64,48,128]{2,1,0:T(8,128)(2,1)S(1)} %reshape.108), channel_id=1, replica_groups=mesh['dp'=4,'expert'=64] {'expert'}, dimensions={0} | all-to-all | bytes 1572864 | tf_op jit(solution)/shard_map/all_to_all | solution.py:34
  157.1 4.1 %fusion.18 = f32[768,192]{0,1:T(8,128)} fusion(bf16[768,2048]{1,0:T(8,128)(2,1)} %all-gather.9.cloned.1.call-done, bf16[1,4096,192]{1,2,0:T(8,128)(2,1)S(1)} %copy-done.12), kind=kOutput, calls=%fused_computation.42 | convolution fusion | flops 603979776 | bytes 4521984 | tf_op jit(solution)/shard_map/dot_general | solution.py:69
  163.3 4.4 %convolution_add_fusion = f32[768,192]{0,1:T(8,128)} fusion(f32[768,192]{0,1:T(8,128)} %fusion.18, bf16[768,2048]{1,0:T(8,128)(2,1)} %all-gather.11.cloned.1.call-done, bf16[1,4096,192]{1,2,0:T(8,128)(2,1)} %param.11), kind=kOutput, calls=%fused_computation.27 | convolution fusion | flops 604127232 | bytes 5111808 | tf_op jit(solution)/shard_map/dot_general | solution.py:69
  169.7 8.5 %all-gather.5.cloned.1.call-done = bf16[768,2176]{1,0:T(8,128)(2,1)} async-done(((bf16[192,2176]{1,0:T(8,128)(2,1)}), bf16[768,2176]{1,0:T(8,128)(2,1)}) %all-gather.5.cloned.1.call-update) | async-done | bytes 3342352 | tf_op jit(solution)/shard_map/all_gather | solution.py:58
  179.3 4.1 %fusion.5 = f32[768,192]{0,1:T(8,128)} fusion(bf16[768,2176]{1,0:T(8,128)(2,1)} %all-gather.5.cloned.1.call-done, bf16[192,4096]{1,0:T(8,128)(2,1)} %bitcast.64), kind=kOutput, calls=%fused_computation.10 | convolution fusion | flops 603979776 | bytes 4521984 | tf_op jit(solution)/shard_map/dot_general | solution.py:82
  183.4 39.4 %all-gather.7.cloned.1.call-done = bf16[768,2048]{1,0:T(8,128)(2,1)} async-done(((bf16[192,2048]{1,0:T(8,128)(2,1)}), bf16[768,2048]{1,0:T(8,128)(2,1)}) %all-gather.7.cloned.1.call-update) | async-done | bytes 3145744 | tf_op jit(solution)/shard_map/all_gather | solution.py:58
  222.7 4.8 %multiply_reduce_fusion = (bf16[768]{0:T(1024)(128)(2,1)S(1)}, bf16[768,192]{0,1:T(8,128)(2,1)}, bf16[768,192]{0,1:T(8,128)(2,1)S(1)}, bf16[768,192]{0,1:T(8,128)(2,1)S(1)}) fusion(f32[768,192]{0,1:T(8,128)} %convolution_add_fusion.1, f32[768,192]{0,1:T(8,128)} %convolution_add_fusion, f32[768]{0:T(1024)S(1)} %convert_reduce_fusion, f32[768,192]{0,1:T(8,128)} %fusion.5, ...), kind=kOutput, calls=%fused_computation.57 | convolution fusion | flops 606928128 | bytes 6590976 | tf_op jit(solution)/shard_map/dot_general | solution.py:82
  232.4 2.3 fusion.13
  234.7 2.7 add_convert_fusion
  237.4 37.8 %reduce-scatter.3.cloned.1.call-done = bf16[192,2176]{1,0:T(8,128)(2,1)} async-done(((bf16[768,2176]{1,0:T(8,128)(2,1)}), bf16[192,2176]{1,0:T(8,128)(2,1)}) %reduce-scatter.3.cloned.1.call-update) | async-done | bytes 835600 | tf_op jit(solution)/shard_map/reduce_scatter | solution.py:116
  276.9 10.8 %all-to-all-start.7 = ((bf16[64,1,3]{2,1,0:T(2,128)(2,1)}), bf16[64,1,3]{2,1,0:T(2,128)(2,1)S(1)}, u32[]{:S(2)}, u32[]{:S(2)}) async-start(bf16[64,1,3]{2,1,0:T(2,128)(2,1)} %all_to_all.41), calls=%async_computation.9 | async-start | bytes 65536 | tf_op jit(solution)/shard_map/all_to_all | solution.py:119
  287.7 30.6 %reduce-scatter.5.cloned.1.call-done = bf16[192,2048]{1,0:T(8,128)(2,1)} async-done(((bf16[768,2048]{1,0:T(8,128)(2,1)}), bf16[192,2048]{1,0:T(8,128)(2,1)}) %reduce-scatter.5.cloned.1.call-update) | async-done | bytes 786448 | tf_op jit(solution)/shard_map/reduce_scatter | solution.py:116
  320.4 10.9 %all-to-all-start.6 = ((bf16[64,48,128]{2,1,0:T(8,128)(2,1)}), bf16[64,48,128]{2,1,0:T(8,128)(2,1)}, u32[]{:S(2)}, u32[]{:S(2)}) async-start(bf16[64,48,128]{2,1,0:T(8,128)(2,1)} %reshape.116), calls=%async_computation.8 | async-start | bytes 1572864 | tf_op jit(solution)/shard_map/all_to_all | solution.py:34
  331.4 3.7 convolution_convert_fusion.3
  343.6 2.2 reshape.114
  345.8 8.5 %all-to-all-done.6 = bf16[64,48,128]{2,1,0:T(8,128)(2,1)} async-done(((bf16[64,48,128]{2,1,0:T(8,128)(2,1)}), bf16[64,48,128]{2,1,0:T(8,128)(2,1)}, u32[]{:S(2)}, u32[]{:S(2)}) %all-to-all-start.6) | async-done | bytes 786464 | tf_op jit(solution)/shard_map/all_to_all | solution.py:34
  354.3 6.1 %all-to-all-start.5 = ((bf16[64,48,128]{2,1,0:T(8,128)(2,1)}), bf16[64,48,128]{2,1,0:T(8,128)(2,1)}, u32[]{:S(2)}, u32[]{:S(2)}) async-start(bf16[64,48,128]{2,1,0:T(8,128)(2,1)} %reshape.114), calls=%async_computation.6 | async-start | bytes 1572864 | tf_op jit(solution)/shard_map/all_to_all | solution.py:34
  367.7 15.6 %all-to-all-done.5 = bf16[64,48,128]{2,1,0:T(8,128)(2,1)} async-done(((bf16[64,48,128]{2,1,0:T(8,128)(2,1)}), bf16[64,48,128]{2,1,0:T(8,128)(2,1)}, u32[]{:S(2)}, u32[]{:S(2)}) %all-to-all-start.5) | async-done | bytes 786464 | tf_op jit(solution)/shard_map/all_to_all | solution.py:34
  (118 shorter events, 47.6 us)
Async XLA Ops:
  7.2 72.3 %copy-start = (bf16[128,1]{0,1:T(2,128)(2,1)S(1)}, bf16[128,1]{0,1:T(2,128)(2,1)}, u32[]{:S(2)}) copy-start(bf16[128,1]{0,1:T(2,128)(2,1)} %param.10) | copy-start | bytes 772
  7.2 149.9 %all-gather.9.cloned.1.call-start = ((), (), s32[]{:S(2)}) async-start(), calls=%async_computation.12 | async-start | bytes 3932160 | tf_op jit(solution)/shard_map/all_gather | solution.py:49
  9.6 39.1 %copy-start.18 = (bf16[128,4096]{1,0:T(8,128)(2,1)S(1)}, bf16[128,4096]{1,0:T(8,128)(2,1)}, u32[]{:S(2)}) copy-start(bf16[128,4096]{1,0:T(8,128)(2,1)} %param.7) | copy-start | bytes 3145732
  48.7 114.6 %all-gather.11.cloned.1.call-start = ((), (), s32[]{:S(2)}) async-start(), calls=%async_computation.13 | async-start | bytes 3932160 | tf_op jit(solution)/shard_map/all_gather | solution.py:49
  49.1 37.2 %copy-start.19 = (bf16[128,4096]{1,0:T(8,128)(2,1)S(1)}, bf16[128,4096]{1,0:T(8,128)(2,1)}, u32[]{:S(2)}) copy-start(bf16[128,4096]{1,0:T(8,128)(2,1)} %param.8) | copy-start | bytes 3145732
  80.4 15.2 %all-to-all-start.1 = ((bf16[64,1,3]{2,1,0:T(2,128)(2,1)}), bf16[64,1,3]{2,1,0:T(2,128)(2,1)S(1)}, u32[]{:S(2)}, u32[]{:S(2)}) async-start(bf16[64,1,3]{2,1,0:T(2,128)(2,1)} %all_to_all.40), calls=%async_computation.1 | async-start | bytes 65536 | tf_op jit(solution)/shard_map/all_to_all | solution.py:46
  95.7 27.9 %all-to-all-start = ((bf16[64,48,128]{2,1,0:T(8,128)(2,1)}), bf16[64,48,128]{2,1,0:T(8,128)(2,1)S(1)}, u32[]{:S(2)}, u32[]{:S(2)}) async-start(bf16[64,48,128]{2,1,0:T(8,128)(2,1)} %reshape.105), calls=%async_computation | async-start | bytes 1572864 | tf_op jit(solution)/shard_map/all_to_all | solution.py:34
  100.4 77.8 %all-gather.5.cloned.1.call-start = ((), (), s32[]{:S(2)}) async-start(), calls=%async_computation.10 | async-start | bytes 4177920 | tf_op jit(solution)/shard_map/all_gather | solution.py:58
  125.0 32.1 %copy-start.12 = (bf16[1,4096,192]{1,2,0:T(8,128)(2,1)S(1)}, bf16[1,4096,192]{1,2,0:T(8,128)(2,1)}, u32[]{:S(2)}) copy-start(bf16[1,4096,192]{1,2,0:T(8,128)(2,1)} %param.11) | copy-start | bytes 4718596
  125.0 97.7 %all-gather.7.cloned.1.call-start = ((), (), s32[]{:S(2)}) async-start(), calls=%async_computation.11 | async-start | bytes 3932160 | tf_op jit(solution)/shard_map/all_gather | solution.py:58
  156.8 4.4 %copy-start.14 = (bf16[1,4096,192]{1,2,0:T(8,128)(2,1)S(1)}, bf16[1,4096,192]{1,2,0:T(8,128)(2,1)}, u32[]{:S(2)}) copy-start(bf16[1,4096,192]{1,2,0:T(8,128)(2,1)} %param.12) | copy-start | bytes 4718596
  156.9 118.4 %reduce-scatter.3.cloned.1.call-start = ((), (), s32[]{:S(2)}) async-start(), calls=%async_computation.14 | async-start | bytes 4177920 | tf_op jit(solution)/shard_map/reduce_scatter | solution.py:116
  157.1 4.1 %copy-start.3 = (bf16[768,2048]{1,0:T(8,128)(2,1)S(1)}, bf16[768,2048]{1,0:T(8,128)(2,1)}, u32[]{:S(2)}) copy-start(bf16[768,2048]{1,0:T(8,128)(2,1)} %all-gather.9.cloned.1.call-done) | copy-start | bytes 9437188
  163.3 4.4 %copy-start.2 = (bf16[768,2048]{1,0:T(8,128)(2,1)S(1)}, bf16[768,2048]{1,0:T(8,128)(2,1)}, u32[]{:S(2)}) copy-start(bf16[768,2048]{1,0:T(8,128)(2,1)} %all-gather.11.cloned.1.call-done) | copy-start | bytes 9437188
  163.3 4.4 %copy-start.15 = (bf16[1,4096,192]{1,2,0:T(8,128)(2,1)S(1)}, bf16[1,4096,192]{1,2,0:T(8,128)(2,1)}, u32[]{:S(2)}) copy-start(bf16[1,4096,192]{1,2,0:T(8,128)(2,1)} %param.12) | copy-start | bytes 4718596
  163.3 4.4 %copy-start.25 = (f32[768,192]{0,1:T(8,128)S(1)}, f32[768,192]{0,1:T(8,128)}, u32[]{:S(2)}) copy-start(f32[768,192]{0,1:T(8,128)} %fusion.23) | copy-start | bytes 1769476
  222.7 4.8 %copy-start.13 = (bf16[1,4096,192]{1,2,0:T(8,128)(2,1)S(1)}, bf16[1,4096,192]{1,2,0:T(8,128)(2,1)}, u32[]{:S(2)}) copy-start(bf16[1,4096,192]{1,2,0:T(8,128)(2,1)} %param.11) | copy-start | bytes 4718596
  232.3 85.9 %reduce-scatter.5.cloned.1.call-start = ((), (), s32[]{:S(2)}) async-start(), calls=%async_computation.15 | async-start | bytes 3932160 | tf_op jit(solution)/shard_map/reduce_scatter | solution.py:116
  276.9 43.5 %all-to-all-start.7 = ((bf16[64,1,3]{2,1,0:T(2,128)(2,1)}), bf16[64,1,3]{2,1,0:T(2,128)(2,1)S(1)}, u32[]{:S(2)}, u32[]{:S(2)}) async-start(bf16[64,1,3]{2,1,0:T(2,128)(2,1)} %all_to_all.41), calls=%async_computation.9 | async-start | bytes 65536 | tf_op jit(solution)/shard_map/all_to_all | solution.py:119
  320.4 33.9 %all-to-all-start.6 = ((bf16[64,48,128]{2,1,0:T(8,128)(2,1)}), bf16[64,48,128]{2,1,0:T(8,128)(2,1)}, u32[]{:S(2)}, u32[]{:S(2)}) async-start(bf16[64,48,128]{2,1,0:T(8,128)(2,1)} %reshape.116), calls=%async_computation.8 | async-start | bytes 1572864 | tf_op jit(solution)/shard_map/all_to_all | solution.py:34
  331.3 3.7 copy-start.4
  342.6 17.8 %copy-start.8 = (bf16[768,192]{0,1:T(8,128)(2,1)S(1)}, bf16[768,192]{0,1:T(8,128)(2,1)}, u32[]{:S(2)}) copy-start(bf16[768,192]{0,1:T(8,128)(2,1)} %copy-done.5) | copy-start | bytes 884740
  354.3 29.0 %all-to-all-start.5 = ((bf16[64,48,128]{2,1,0:T(8,128)(2,1)}), bf16[64,48,128]{2,1,0:T(8,128)(2,1)}, u32[]{:S(2)}, u32[]{:S(2)}) async-start(bf16[64,48,128]{2,1,0:T(8,128)(2,1)} %reshape.114), calls=%async_computation.6 | async-start | bytes 1572864 | tf_op jit(solution)/shard_map/all_to_all | solution.py:34
  365.9 20.2 %copy-start.1 = (bf16[128,1]{0,1:T(2,128)(2,1)S(1)}, bf16[128,1]{0,1:T(2,128)(2,1)}, u32[]{:S(2)}) copy-start(bf16[128,1]{0,1:T(2,128)(2,1)} %param.10) | copy-start | bytes 772
  (14 other events, 29.7 us)
Sparse Core Ops, SparseCore 0:
  48.8 38.3 all-gather.8
  89.6 42.2 all-gather.10
  134.3 43.8 all-gather.4
  180.4 42.2 all-gather.6
  232.5 42.7 reduce-scatter.2
  277.6 40.5 reduce-scatter.4
where the time goes:
time: 394 us; the launch traced here: 393 us
  waiting for transfers between devices  171 us (43%)
  blocking collectives  93.3 us (24%)
  matrix products  45.1 us (11%)
  starting transfers between devices  38.8 us (10%)
  local copies, waits for them, and re-layouts  19.2 us (5%)
  between operations  14.5 us (4%)
  other arithmetic  11 us (3%)
    all_to_all x3, blocking collectives, to_expert(): lax.all_to_all(shaped, 'expert', 0, 0, tiled=True)  93.3 us
    reduce_scatter x2, waiting for transfers between devices, body(): lax.psum_scatter(part.astype(jnp.bfloat16), 'dp', scatter_dimension=0, ti...  68.4 us
    all_gather x2, waiting for transfers between devices, body(): gathered = lax.all_gather(recv, 'dp', axis=0, tiled=True)  47.9 us
    all_to_all x3, waiting for transfers between devices, to_expert(): lax.all_to_all(shaped, 'expert', 0, 0, tiled=True)  46.9 us
    all_to_all x3, starting transfers between devices, to_expert(): lax.all_to_all(shaped, 'expert', 0, 0, tiled=True)  21.7 us
    all_to_all x1, starting transfers between devices, body(): lax.all_to_all(own_scores, 'expert', 0, 0, tiled=True).reshape(slot_total)  10.8 us
    dot_general x2, matrix products, body(): lax.dot_general(rows_dy[c], down_w[:, c * piece:(c + 1) * piece], contrac...  8.91 us
    dot_general x2, matrix products, body(): jnp.dot(rows_in[c], gate_w[c * piece:(c + 1) * piece], preferred_element_...  8.5 us
  transfers between devices with their start and end apart: 11, of which 8 were waited for; matrix products, arithmetic and copies ran while one was open for 14% of the time, Pallas kernels for 0%

commit v1 on v0

--- a/solution.py
+++ b/solution.py
@@ -5,6 +5,13 @@
 
 LANES = 128
 CHUNKS = 2
+
+
+def swapped_in(value, axis, d):
+    devices = lax.axis_size(axis)
+    blocks = jnp.stack([value for _ in range(devices)])
+    blocks = lax.all_to_all(blocks, axis, split_axis=0, concat_axis=0)
+    return jnp.concatenate(blocks, axis=d)
 
 
 def body(tokens, out_grad, routes, gate_probs, w_gate, w_up, w_down):
@@ -55,7 +62,7 @@
             recv = jnp.concatenate(
                 [recv, jnp.broadcast_to(recv_prob[:, None], (slot_total, LANES))], axis=1
             )
-        gathered = lax.all_gather(recv, "dp", axis=0, tiled=True)
+        gathered = swapped_in(recv, "dp", 0)
         if c == 0:
             rows_prob = gathered[:, piece]
             gathered = gathered[:, :piece]

time: 394 us -> 426 us (1.081)
  waiting for transfers between devices: 171 us -> 234 us
  blocking collectives: 93.3 us -> 35.9 us
  starting transfers between devices: 38.8 us -> 59.2 us
  local copies, waits for them, and re-layouts: 19.2 us -> 27.8 us
    all_to_all x0 -> x2, waiting for transfers between devices: none -> 71.3 us  [swapped_in(): blocks = lax.all_to_all(blocks, axis, split_axis=0, concat_axis=0)]
    all_to_all x3 -> x1, blocking collectives: 93.3 us -> 35.9 us  [to_expert(): lax.all_to_all(shaped, 'expert', 0, 0, tiled=True)]
    all_gather x2 -> x0, waiting for transfers between devices: 47.9 us -> none  [body(): gathered = lax.all_gather(recv, 'dp', axis=0, tiled=True)]
    all_to_all x3 -> x5, waiting for transfers between devices: 46.9 us -> 86.7 us  [to_expert(): lax.all_to_all(shaped, 'expert', 0, 0, tiled=True)]
    all_to_all x3 -> x5, starting transfers between devices: 21.7 us -> 33.5 us  [to_expert(): lax.all_to_all(shaped, 'expert', 0, 0, tiled=True)]
    all_to_all x0 -> x2, starting transfers between devices: none -> 8.68 us  [swapped_in(): blocks = lax.all_to_all(blocks, axis, split_axis=0, concat_axis=0)]
    another operation x0 -> x3, local copies, waits for them, and re-layouts: none -> 7.83 us  [swapped_in(): blocks = jnp.stack([value for _ in range(devices)])]
  transfers between devices with their start and end apart: 11 -> 13, of which waited for: 8 -> 10; matrix products, arithmetic and copies ran while one was open for 14% -> 14% of each run, Pallas kernels for 0% -> 0%
where the time goes in v1:
time: 426 us; the launch traced here: 425 us
  waiting for transfers between devices  234 us (55%)
  starting transfers between devices  59.2 us (14%)
  matrix products  44.1 us (10%)
  blocking collectives  35.9 us (8%)
  local copies, waits for them, and re-layouts  27.8 us (7%)
  between operations  14.2 us (3%)
  other arithmetic  9.17 us (2%)
    all_to_all x5, waiting for transfers between devices, to_expert(): lax.all_to_all(shaped, 'expert', 0, 0, tiled=True)  86.7 us
    all_to_all x2, waiting for transfers between devices, swapped_in(): blocks = lax.all_to_all(blocks, axis, split_axis=0, concat_axis=0)  71.3 us
    reduce_scatter x2, waiting for transfers between devices, body(): lax.psum_scatter(part.astype(jnp.bfloat16), 'dp', scatter_dimension=0, ti...  68.5 us
    all_to_all x1, blocking collectives, to_expert(): lax.all_to_all(shaped, 'expert', 0, 0, tiled=True)  35.9 us
    all_to_all x5, starting transfers between devices, to_expert(): lax.all_to_all(shaped, 'expert', 0, 0, tiled=True)  33.5 us
    all_to_all x1, starting transfers between devices, body(): lax.all_to_all(own_scores, 'expert', 0, 0, tiled=True).reshape(slot_total)  10.7 us
    reshape x6, local copies, waits for them, and re-layouts, to_expert(): shaped = rows.reshape(expert_count, per_peer, LANES)  8.77 us
    all_to_all x2, starting transfers between devices, swapped_in(): blocks = lax.all_to_all(blocks, axis, split_axis=0, concat_axis=0)  8.68 us
  transfers between devices with their start and end apart: 13, of which 10 were waited for; matrix products, arithmetic and copies ran while one was open for 14% of the time, Pallas kernels for 0%

profile of v1, /device:TPU:1, one launch (start us, length us, event | category | flops | bytes accessed | tf_op | source)
XLA Modules:
  0.0 424.7 jit_solution(16709124078026857130)
XLA Ops:
  11.4 35.9 %all_to_all.60 = bf16[64,48,128]{2,1,0:T(8,128)(2,1)S(1)} all-to-all(bf16[64,48,128]{2,1,0:T(8,128)(2,1)S(1)} %reshape.118), channel_id=1, replica_groups=mesh['dp'=4,'expert'=64] {'expert'}, dimensions={0} | all-to-all | bytes 1572864 | tf_op jit(solution)/shard_map/all_to_all | solution.py:41
  49.6 5.9 %all-to-all-start.1 = ((bf16[64,1,3]{2,1,0:T(2,128)(2,1)}), bf16[64,1,3]{2,1,0:T(2,128)(2,1)S(1)}, u32[]{:S(2)}, u32[]{:S(2)}) async-start(bf16[64,1,3]{2,1,0:T(2,128)(2,1)} %all_to_all.48), calls=%async_computation.1 | async-start | bytes 65536 | tf_op jit(solution)/shard_map/all_to_all | solution.py:53
  57.1 7.7 %all-to-all-done.1 = bf16[64,1,3]{2,1,0:T(2,128)(2,1)S(1)} async-done(((bf16[64,1,3]{2,1,0:T(2,128)(2,1)}), bf16[64,1,3]{2,1,0:T(2,128)(2,1)S(1)}, u32[]{:S(2)}, u32[]{:S(2)}) %all-to-all-start.1) | async-done | bytes 416 | tf_op jit(solution)/shard_map/all_to_all | solution.py:53
  64.8 4.8 %all-to-all-start.6 = ((bf16[64,48,128]{2,1,0:T(8,128)(2,1)}), bf16[64,48,128]{2,1,0:T(8,128)(2,1)S(1)}, u32[]{:S(2)}, u32[]{:S(2)}) async-start(bf16[64,48,128]{2,1,0:T(8,128)(2,1)} %reshape.120), calls=%async_computation.6 | async-start | bytes 1572864 | tf_op jit(solution)/shard_map/all_to_all | solution.py:41
  72.2 20.5 %all-to-all-done.6 = bf16[64,48,128]{2,1,0:T(8,128)(2,1)S(1)} async-done(((bf16[64,48,128]{2,1,0:T(8,128)(2,1)}), bf16[64,48,128]{2,1,0:T(8,128)(2,1)S(1)}, u32[]{:S(2)}, u32[]{:S(2)}) %all-to-all-start.6) | async-done | bytes 786464 | tf_op jit(solution)/shard_map/all_to_all | solution.py:41
  92.8 5.8 %all-to-all-start = ((bf16[64,48,128]{2,1,0:T(8,128)(2,1)}), bf16[64,48,128]{2,1,0:T(8,128)(2,1)S(1)}, u32[]{:S(2)}, u32[]{:S(2)}) async-start(bf16[64,48,128]{2,1,0:T(8,128)(2,1)} %reshape.112), calls=%async_computation | async-start | bytes 1572864 | tf_op jit(solution)/shard_map/all_to_all | solution.py:41
  100.2 21.4 %all-to-all-done = bf16[64,48,128]{2,1,0:T(8,128)(2,1)S(1)} async-done(((bf16[64,48,128]{2,1,0:T(8,128)(2,1)}), bf16[64,48,128]{2,1,0:T(8,128)(2,1)S(1)}, u32[]{:S(2)}, u32[]{:S(2)}) %all-to-all-start) | async-done | bytes 786464 | tf_op jit(solution)/shard_map/all_to_all | solution.py:41
  121.6 5.9 %all-to-all-start.3 = ((bf16[64,48,128]{2,1,0:T(8,128)(2,1)}), bf16[64,48,128]{2,1,0:T(8,128)(2,1)S(1)}, u32[]{:S(2)}, u32[]{:S(2)}) async-start(bf16[64,48,128]{2,1,0:T(8,128)(2,1)} %reshape.116), calls=%async_computation.3 | async-start | bytes 1572864 | tf_op jit(solution)/shard_map/all_to_all | solution.py:41
  129.6 21.0 %all-to-all-done.3 = bf16[64,48,128]{2,1,0:T(8,128)(2,1)S(1)} async-done(((bf16[64,48,128]{2,1,0:T(8,128)(2,1)}), bf16[64,48,128]{2,1,0:T(8,128)(2,1)S(1)}, u32[]{:S(2)}, u32[]{:S(2)}) %all-to-all-start.3) | async-done | bytes 786464 | tf_op jit(solution)/shard_map/all_to_all | solution.py:41
  152.5 4.0 all-to-all-start.2
  158.7 50.6 %all-to-all-done.2 = bf16[4,192,2176]{2,1,0:T(8,128)(2,1)S(1)} async-done(((bf16[4,192,2176]{2,1,0:T(8,128)(2,1)}), bf16[4,192,2176]{2,1,0:T(8,128)(2,1)S(1)}, u32[]{:S(2)}, u32[]{:S(2)}) %all-to-all-start.2) | async-done | bytes 3342368 | tf_op jit(solution)/shard_map/all_to_all | solution.py:13
  213.0 4.7 %all-to-all-start.4 = ((bf16[4,192,2048]{2,1,0:T(8,128)(2,1)}), bf16[4,192,2048]{2,1,0:T(8,128)(2,1)}, u32[]{:S(2)}, u32[]{:S(2)}) async-start(bf16[4,192,2048]{2,1,0:T(8,128)(2,1)} %stack.5), calls=%async_computation.4 | async-start | bytes 6291456 | tf_op jit(solution)/shard_map/all_to_all | solution.py:13
  221.2 4.2 fusion.18
  227.5 4.4 %convolution_add_fusion = f32[768,192]{0,1:T(8,128)} fusion(f32[768,192]{0,1:T(8,128)} %fusion.18, bf16[768,2048]{1,0:T(8,128)(2,1)} %all-gather.5.cloned.1.call-done, bf16[1,4096,192]{1,2,0:T(8,128)(2,1)} %param.11), kind=kOutput, calls=%fused_computation.27 | convolution fusion | flops 604127232 | bytes 5111808 | tf_op jit(solution)/shard_map/dot_general | solution.py:76
  233.9 20.7 %all-to-all-done.4 = bf16[4,192,2048]{2,1,0:T(8,128)(2,1)} async-done(((bf16[4,192,2048]{2,1,0:T(8,128)(2,1)}), bf16[4,192,2048]{2,1,0:T(8,128)(2,1)}, u32[]{:S(2)}, u32[]{:S(2)}) %all-to-all-start.4) | async-done | bytes 3145760 | tf_op jit(solution)/shard_map/all_to_all | solution.py:13
  254.6 4.8 %multiply_reduce_fusion = (bf16[768]{0:T(1024)(128)(2,1)S(1)}, bf16[768,192]{0,1:T(8,128)(2,1)}, bf16[768,192]{0,1:T(8,128)(2,1)S(1)}, bf16[768,192]{0,1:T(8,128)(2,1)S(1)}) fusion(f32[768,192]{0,1:T(8,128)} %convolution_add_fusion.1, f32[768,192]{0,1:T(8,128)} %convolution_add_fusion, f32[768]{0:T(1024)S(1)} %convert_reduce_fusion, f32[768,192]{0,1:T(8,128)} %fusion.5, ...), kind=kOutput, calls=%fused_computation.57 | convolution fusion | flops 606928128 | bytes 6590976 | tf_op jit(solution)/shard_map/dot_general | solution.py:89
  269.3 38.0 %reduce-scatter.3.cloned.1.call-done = bf16[192,2176]{1,0:T(8,128)(2,1)} async-done(((bf16[768,2176]{1,0:T(8,128)(2,1)}), bf16[192,2176]{1,0:T(8,128)(2,1)}) %reduce-scatter.3.cloned.1.call-update) | async-done | bytes 835600 | tf_op jit(solution)/shard_map/reduce_scatter | solution.py:123
  309.0 10.7 %all-to-all-start.9 = ((bf16[64,1,3]{2,1,0:T(2,128)(2,1)}), bf16[64,1,3]{2,1,0:T(2,128)(2,1)S(1)}, u32[]{:S(2)}, u32[]{:S(2)}) async-start(bf16[64,1,3]{2,1,0:T(2,128)(2,1)} %all_to_all.49), calls=%async_computation.11 | async-start | bytes 65536 | tf_op jit(solution)/shard_map/all_to_all | solution.py:126
  319.7 30.5 %reduce-scatter.5.cloned.1.call-done = bf16[192,2048]{1,0:T(8,128)(2,1)} async-done(((bf16[768,2048]{1,0:T(8,128)(2,1)}), bf16[192,2048]{1,0:T(8,128)(2,1)}) %reduce-scatter.5.cloned.1.call-update) | async-done | bytes 786448 | tf_op jit(solution)/shard_map/reduce_scatter | solution.py:123
  352.4 10.9 %all-to-all-start.8 = ((bf16[64,48,128]{2,1,0:T(8,128)(2,1)}), bf16[64,48,128]{2,1,0:T(8,128)(2,1)}, u32[]{:S(2)}, u32[]{:S(2)}) async-start(bf16[64,48,128]{2,1,0:T(8,128)(2,1)} %reshape.124), calls=%async_computation.10 | async-start | bytes 1572864 | tf_op jit(solution)/shard_map/all_to_all | solution.py:41
  368.9 3.8 fusion.8
  378.1 8.2 %all-to-all-done.8 = bf16[64,48,128]{2,1,0:T(8,128)(2,1)} async-done(((bf16[64,48,128]{2,1,0:T(8,128)(2,1)}), bf16[64,48,128]{2,1,0:T(8,128)(2,1)}, u32[]{:S(2)}, u32[]{:S(2)}) %all-to-all-start.8) | async-done | bytes 786464 | tf_op jit(solution)/shard_map/all_to_all | solution.py:41
  386.3 6.1 %all-to-all-start.7 = ((bf16[64,48,128]{2,1,0:T(8,128)(2,1)}), bf16[64,48,128]{2,1,0:T(8,128)(2,1)}, u32[]{:S(2)}, u32[]{:S(2)}) async-start(bf16[64,48,128]{2,1,0:T(8,128)(2,1)} %reshape.122), calls=%async_computation.8 | async-start | bytes 1572864 | tf_op jit(solution)/shard_map/all_to_all | solution.py:41
  399.8 15.6 %all-to-all-done.7 = bf16[64,48,128]{2,1,0:T(8,128)(2,1)} async-done(((bf16[64,48,128]{2,1,0:T(8,128)(2,1)}), bf16[64,48,128]{2,1,0:T(8,128)(2,1)}, u32[]{:S(2)}, u32[]{:S(2)}) %all-to-all-start.7) | async-done | bytes 786464 | tf_op jit(solution)/shard_map/all_to_all | solution.py:41
  (122 shorter events, 64.2 us)
Async XLA Ops:
  7.2 41.4 %copy-start = (bf16[128,1]{0,1:T(2,128)(2,1)S(1)}, bf16[128,1]{0,1:T(2,128)(2,1)}, u32[]{:S(2)}) copy-start(bf16[128,1]{0,1:T(2,128)(2,1)} %param.10) | copy-start | bytes 772
  7.2 214.0 %all-gather.3.cloned.1.call-start = ((), (), s32[]{:S(2)}) async-start(), calls=%async_computation.12 | async-start | bytes 3932160 | tf_op jit(solution)/shard_map/all_gather | solution.py:56
  11.0 44.5 %copy-start.21 = (bf16[128,4096]{1,0:T(8,128)(2,1)S(1)}, bf16[128,4096]{1,0:T(8,128)(2,1)}, u32[]{:S(2)}) copy-start(bf16[128,4096]{1,0:T(8,128)(2,1)} %param.7) | copy-start | bytes 3145732
  49.6 15.2 %all-to-all-start.1 = ((bf16[64,1,3]{2,1,0:T(2,128)(2,1)}), bf16[64,1,3]{2,1,0:T(2,128)(2,1)S(1)}, u32[]{:S(2)}, u32[]{:S(2)}) async-start(bf16[64,1,3]{2,1,0:T(2,128)(2,1)} %all_to_all.48), calls=%async_computation.1 | async-start | bytes 65536 | tf_op jit(solution)/shard_map/all_to_all | solution.py:53
  57.1 41.5 %copy-start.22 = (bf16[128,4096]{1,0:T(8,128)(2,1)S(1)}, bf16[128,4096]{1,0:T(8,128)(2,1)}, u32[]{:S(2)}) copy-start(bf16[128,4096]{1,0:T(8,128)(2,1)} %param.8) | copy-start | bytes 3145732
  64.8 27.9 %all-to-all-start.6 = ((bf16[64,48,128]{2,1,0:T(8,128)(2,1)}), bf16[64,48,128]{2,1,0:T(8,128)(2,1)S(1)}, u32[]{:S(2)}, u32[]{:S(2)}) async-start(bf16[64,48,128]{2,1,0:T(8,128)(2,1)} %reshape.120), calls=%async_computation.6 | async-start | bytes 1572864 | tf_op jit(solution)/shard_map/all_to_all | solution.py:41
  92.8 28.9 %all-to-all-start = ((bf16[64,48,128]{2,1,0:T(8,128)(2,1)}), bf16[64,48,128]{2,1,0:T(8,128)(2,1)S(1)}, u32[]{:S(2)}, u32[]{:S(2)}) async-start(bf16[64,48,128]{2,1,0:T(8,128)(2,1)} %reshape.112), calls=%async_computation | async-start | bytes 1572864 | tf_op jit(solution)/shard_map/all_to_all | solution.py:41
  121.6 28.9 %all-to-all-start.3 = ((bf16[64,48,128]{2,1,0:T(8,128)(2,1)}), bf16[64,48,128]{2,1,0:T(8,128)(2,1)S(1)}, u32[]{:S(2)}, u32[]{:S(2)}) async-start(bf16[64,48,128]{2,1,0:T(8,128)(2,1)} %reshape.116), calls=%async_computation.3 | async-start | bytes 1572864 | tf_op jit(solution)/shard_map/all_to_all | solution.py:41
  127.5 99.9 %all-gather.5.cloned.1.call-start = ((), (), s32[]{:S(2)}) async-start(), calls=%async_computation.13 | async-start | bytes 3932160 | tf_op jit(solution)/shard_map/all_gather | solution.py:56
  152.5 56.8 %all-to-all-start.2 = ((bf16[4,192,2176]{2,1,0:T(8,128)(2,1)}), bf16[4,192,2176]{2,1,0:T(8,128)(2,1)S(1)}, u32[]{:S(2)}, u32[]{:S(2)}) async-start(bf16[4,192,2176]{2,1,0:T(8,128)(2,1)} %stack.4), calls=%async_computation.2 | async-start | bytes 6684672 | tf_op jit(solution)/shard_map/all_to_all | solution.py:13
  209.3 8.8 %copy-start.10 = (bf16[4,192,2176]{2,1,0:T(8,128)(2,1)}, bf16[4,192,2176]{2,1,0:T(8,128)(2,1)S(1)}, u32[]{:S(2)}) copy-start(bf16[4,192,2176]{2,1,0:T(8,128)(2,1)S(1)} %all-to-all-done.2) | copy-start | bytes 10027012
  213.0 41.6 %all-to-all-start.4 = ((bf16[4,192,2048]{2,1,0:T(8,128)(2,1)}), bf16[4,192,2048]{2,1,0:T(8,128)(2,1)}, u32[]{:S(2)}, u32[]{:S(2)}) async-start(bf16[4,192,2048]{2,1,0:T(8,128)(2,1)} %stack.5), calls=%async_computation.4 | async-start | bytes 6291456 | tf_op jit(solution)/shard_map/all_to_all | solution.py:13
  217.7 89.6 %reduce-scatter.3.cloned.1.call-start = ((), (), s32[]{:S(2)}) async-start(), calls=%async_computation.14 | async-start | bytes 4177920 | tf_op jit(solution)/shard_map/reduce_scatter | solution.py:123
  227.5 4.4 %copy-start.3 = (bf16[768,2048]{1,0:T(8,128)(2,1)S(1)}, bf16[768,2048]{1,0:T(8,128)(2,1)}, u32[]{:S(2)}) copy-start(bf16[768,2048]{1,0:T(8,128)(2,1)} %all-gather.5.cloned.1.call-done) | copy-start | bytes 9437188
  227.5 4.4 %copy-start.18 = (bf16[1,4096,192]{1,2,0:T(8,128)(2,1)S(1)}, bf16[1,4096,192]{1,2,0:T(8,128)(2,1)}, u32[]{:S(2)}) copy-start(bf16[1,4096,192]{1,2,0:T(8,128)(2,1)} %param.12) | copy-start | bytes 4718596
  227.5 4.4 %copy-start.26 = (f32[768,192]{0,1:T(8,128)S(1)}, f32[768,192]{0,1:T(8,128)}, u32[]{:S(2)}) copy-start(f32[768,192]{0,1:T(8,128)} %fusion.23) | copy-start | bytes 1769476
  254.6 4.8 %copy-start.16 = (bf16[1,4096,192]{1,2,0:T(8,128)(2,1)S(1)}, bf16[1,4096,192]{1,2,0:T(8,128)(2,1)}, u32[]{:S(2)}) copy-start(bf16[1,4096,192]{1,2,0:T(8,128)(2,1)} %param.11) | copy-start | bytes 4718596
  264.2 86.1 %reduce-scatter.5.cloned.1.call-start = ((), (), s32[]{:S(2)}) async-start(), calls=%async_computation.15 | async-start | bytes 3932160 | tf_op jit(solution)/shard_map/reduce_scatter | solution.py:123
  309.0 43.5 %all-to-all-start.9 = ((bf16[64,1,3]{2,1,0:T(2,128)(2,1)}), bf16[64,1,3]{2,1,0:T(2,128)(2,1)S(1)}, u32[]{:S(2)}, u32[]{:S(2)}) async-start(bf16[64,1,3]{2,1,0:T(2,128)(2,1)} %all_to_all.49), calls=%async_computation.11 | async-start | bytes 65536 | tf_op jit(solution)/shard_map/all_to_all | solution.py:126
  352.4 33.9 %all-to-all-start.8 = ((bf16[64,48,128]{2,1,0:T(8,128)(2,1)}), bf16[64,48,128]{2,1,0:T(8,128)(2,1)}, u32[]{:S(2)}, u32[]{:S(2)}) async-start(bf16[64,48,128]{2,1,0:T(8,128)(2,1)} %reshape.124), calls=%async_computation.10 | async-start | bytes 1572864 | tf_op jit(solution)/shard_map/all_to_all | solution.py:41
  374.6 17.8 %copy-start.5 = (bf16[768,2048]{1,0:T(8,128)(2,1)S(1)}, bf16[768,2048]{1,0:T(8,128)(2,1)}, u32[]{:S(2)}) copy-start(bf16[768,2048]{1,0:T(8,128)(2,1)} %all-gather.5.cloned.1.call-done) | copy-start | bytes 9437188
  374.6 17.8 %copy-start.9 = (bf16[768,192]{0,1:T(8,128)(2,1)S(1)}, bf16[768,192]{0,1:T(8,128)(2,1)}, u32[]{:S(2)}) copy-start(bf16[768,192]{0,1:T(8,128)(2,1)} %copy-done.6) | copy-start | bytes 884740
  386.3 29.0 %all-to-all-start.7 = ((bf16[64,48,128]{2,1,0:T(8,128)(2,1)}), bf16[64,48,128]{2,1,0:T(8,128)(2,1)}, u32[]{:S(2)}, u32[]{:S(2)}) async-start(bf16[64,48,128]{2,1,0:T(8,128)(2,1)} %reshape.122), calls=%async_computation.8 | async-start | bytes 1572864 | tf_op jit(solution)/shard_map/all_to_all | solution.py:41
  398.0 20.2 %copy-start.1 = (bf16[128,1]{0,1:T(2,128)(2,1)S(1)}, bf16[128,1]{0,1:T(2,128)(2,1)}, u32[]{:S(2)}) copy-start(bf16[128,1]{0,1:T(2,128)(2,1)} %param.10) | copy-start | bytes 772
  (17 other events, 39.1 us)
Sparse Core Ops, SparseCore 0:
  48.7 38.3 all-gather.2
  130.7 54.8 all-gather.4
  264.3 42.9 reduce-scatter.2
  309.7 40.5 reduce-scatter.4
